TPU v7x, 128 devices: a whole 4x4x4 slice. The times are simulated.
128 devices in a mesh: req: 8 (over x, core), seq: 16 (over z, y).
Axes of the slice: x: 4, y: 4, z: 4, core: 2. Of those that a mesh axis runs over, the one named last changes fastest.
Arguments:
- hidden: bfloat16 [8, 2048, 2048], P('req', 'seq'), may hold values from -6 to 6
- lengths: int32 [8], replicated, may hold values from 1 to 2048, 10240 in all
- slot_request: int32 [8], replicated, may hold values from 0 to 7, each once
- norm_gain: bfloat16 [2048], replicated, may hold values from 0.099609375 to 1.8984375
- in_weight: bfloat16 [2, 2048, 4096], P(None, 'req', 'seq'), may hold values from -0.125 to 0.125
- conv_weight: bfloat16 [4, 4096], P(None, 'seq'), may hold values from -3 to 3
- conv_bias: bfloat16 [4096], P('seq'), may hold values from -0.5 to 0.5
- xproj_weight: bfloat16 [4096, 160], P('seq'), may hold values from -0.09375 to 0.09375
- dt_weight: bfloat16 [128, 4096], P(None, 'seq'), may hold values from -0.5 to 0.5
- dt_bias: bfloat16 [4096], P('seq'), may hold values from -6.91 to -2.25
- a_log: float32 [16, 4096], replicated, may hold values from -2.3 to 1.39
- skip_gain: float32 [4096], replicated, may hold values from 0.5 to 1.5
- out_weight: bfloat16 [4096, 2048], P('seq', 'req'), may hold values from -0.09375 to 0.09375
Outputs:
- mixed: bfloat16 [8, 2048, 2048], P('req', 'seq')
- final_state: float32 [8, 16, 4096], P('req', None, 'seq')
Inputs may be any that keep to these rules, and one draw needn't show every extreme that they name: `lengths`: each slot's length is at least 1, the longest is exactly 2048, and they sum to 10240. `slot_request`: A permutation of the requests.
All inputs are finite; a program needn't handle non-finite values.
Results may differ from a plain program's by a relative error of at most 0.015.
Values may be sent and summed in bfloat16 or wider, within the bound.
No kernel may reach another device: no remote copies, remote signals or barrier semaphores. Data moves between devices by JAX's collectives and lax.ppermute only.
A program may use at most 128 MiB of HBM per device.

v0:
```python
import jax
import jax.numpy as jnp
from jax import lax
from jax.sharding import PartitionSpec as P

STATE = 16
RANK = 128


def shifted(block, axis, distance):
    devices = range(lax.axis_size(axis))
    route = [(i - distance, i) for i in devices if i - distance in devices]
    return lax.ppermute(block, axis, route)


def spread(array, axis, root):
    mine = lax.axis_index(axis) == root
    return lax.psum(jnp.where(mine, array, jnp.zeros_like(array)), axis)


def to_blocks(array):
    pieces, length, columns = array.shape
    return jnp.moveaxis(array.reshape(pieces, 16, length // 16, columns), 1, 0)


def from_blocks(array):
    count, pieces, group, columns = array.shape
    return jnp.moveaxis(array, 0, 1).reshape(pieces, count * group, columns)


def piece_scan(rates, values, entry, readout, decay):
    pieces, length, columns = rates.shape
    group = length // 16
    positions = jnp.arange(length, dtype=jnp.int32)
    lower = (positions[None, :] <= positions[:, None]).astype(jnp.float32)
    running = jnp.einsum("rs,psw->prw", lower, rates, precision=lax.Precision.HIGHEST)

    def advance(state, items):
        rate, value, into, outof = items
        outputs = []
        for place in range(group):
            factor = jnp.exp(rate[:, place][:, None, :] * decay[None])
            state = (
                factor * state
                + (rate[:, place] * value[:, place])[:, None, :] * into[:, place][:, :, None]
            )
            outputs.append(jnp.sum(outof[:, place][:, :, None] * state, axis=1))
        return (state, jnp.stack(outputs, axis=1))

    start = jnp.zeros((pieces, decay.shape[0], columns), jnp.float32)
    end_local, local_out = lax.scan(
        advance, start, (to_blocks(rates), to_blocks(values), to_blocks(entry), to_blocks(readout))
    )
    total_decay = jnp.exp(running[:, length - 1][:, None, :] * decay[None])
    return (end_local, from_blocks(local_out), total_decay, running)


def carried_part(running, readout, decay, carry_in):

    def correct(items):
        total, outof = items
        kept = jnp.exp(total[:, :, None, :] * decay[None, None]) * carry_in[:, None]
        return jnp.sum(outof[:, :, :, None] * kept, axis=2)

    return from_blocks(lax.map(correct, (to_blocks(running), to_blocks(readout))))


def per_device(
    hidden,
    lengths,
    slot_request,
    norm_gain,
    in_weight,
    conv_weight,
    conv_bias,
    xproj_weight,
    dt_weight,
    dt_bias,
    a_log,
    skip_gain,
    out_weight,
):
    seq_count = lax.axis_size("seq")
    seq_index = lax.axis_index("seq")
    req_index = lax.axis_index("req")
    rows = hidden.shape[1]
    span = rows * seq_count
    width = in_weight.shape[2]
    taps_count = conv_weight.shape[0]
    state_count = a_log.shape[0]
    total_inner = a_log.shape[1]
    tokens = hidden[0].astype(jnp.float32)
    scale = lax.rsqrt(jnp.mean(tokens * tokens, axis=-1, keepdims=True) + 1e-05)
    normed = (tokens * scale * norm_gain.astype(jnp.float32)).astype(jnp.bfloat16)
    w_in = lax.all_gather(in_weight, "req", axis=1, tiled=True)
    w_flat = jnp.concatenate((w_in[0], w_in[1]), axis=1)
    both = jnp.dot(
        lax.all_gather(normed, "seq", axis=0, tiled=True),
        w_flat,
        preferred_element_type=jnp.float32,
    )
    xin = both[:, :width]
    zgate = both[:, width:].astype(jnp.bfloat16)
    padded = jnp.pad(xin, ((taps_count - 1, 0), (0, 0)))
    taps = conv_weight.astype(jnp.float32)
    convolved = conv_bias.astype(jnp.float32) + jnp.zeros_like(xin)
    for tap in range(taps_count):
        convolved = convolved + taps[tap] * padded[tap : tap + span, :]
    inner = jax.nn.silu(convolved).astype(jnp.bfloat16)
    partial_proj = jnp.dot(inner, xproj_weight, preferred_element_type=jnp.float32)
    length_here = lax.dynamic_index_in_dim(lengths, req_index, 0, keepdims=False)
    summed = lax.psum(partial_proj, "seq")
    live_all = (jnp.arange(span, dtype=jnp.int32) < length_here).astype(jnp.float32)
    rate_low = summed[:, :RANK].astype(jnp.bfloat16)
    delta_ch = (
        jax.nn.softplus(
            jnp.dot(rate_low, dt_weight, preferred_element_type=jnp.float32)
            + dt_bias.astype(jnp.float32)
        )
        * live_all[:, None]
    )
    w_out = lax.all_gather(out_weight, "req", axis=1, tiled=True)
    inner_tok = lax.all_to_all(inner, "seq", split_axis=0, concat_axis=1, tiled=True)
    delta_tok = lax.all_to_all(
        delta_ch.astype(jnp.bfloat16), "seq", split_axis=0, concat_axis=1, tiled=True
    ).astype(delta_ch.dtype)
    own_proj = lax.dynamic_slice_in_dim(summed, seq_index * rows, rows, 0)
    decay = -jnp.exp(a_log)
    inner_f = inner_tok.astype(jnp.float32)
    entry = own_proj[None, :, RANK : RANK + STATE]
    readout = own_proj[None, :, RANK + STATE :]
    end_local, local_out, total_decay, running = piece_scan(
        delta_tok[None], inner_f[None], entry, readout, decay
    )
    zeros_state = jnp.zeros((state_count, total_inner), jnp.float32)

    def relay(turn, incoming):
        return shifted(total_decay[0] * incoming + end_local[0], "seq", 1)

    carry_in = lax.fori_loop(0, seq_count - 1, relay, zeros_state)
    carried = carried_part(running, readout, decay, carry_in[None])
    scanned = ((local_out + carried)[0] + skip_gain * inner_f).astype(jnp.bfloat16)
    last = spread(
        (total_decay[0] * carry_in + end_local[0]).astype(jnp.bfloat16), "seq", seq_count - 1
    ).astype(jnp.float32)
    mine = lax.dynamic_slice_in_dim(last, seq_index * width, width, 1)
    scanned_ch = lax.all_to_all(scanned, "seq", split_axis=1, concat_axis=0, tiled=True)
    gated_ch = (scanned_ch.astype(jnp.float32) * jax.nn.silu(zgate.astype(jnp.float32))).astype(
        jnp.bfloat16
    )
    branch = lax.psum_scatter(
        jnp.dot(gated_ch, w_out, preferred_element_type=jnp.float32).astype(jnp.bfloat16),
        "seq",
        scatter_dimension=0,
        tiled=True,
    ).astype(jnp.float32)
    slot_all = lax.all_gather(mine[None], "req", axis=0, tiled=True)
    picked = (slot_request == req_index).astype(jnp.float32)
    final_state = jnp.sum(picked[:, None, None] * slot_all, axis=0, keepdims=True)
    mixed = (tokens + branch).astype(jnp.bfloat16)[None]
    return (mixed, final_state)


def solution(mesh):
    in_specs = (
        P("req", "seq", None),
        P(),
        P(),
        P(),
        P(None, "req", "seq"),
        P(None, "seq"),
        P("seq"),
        P("seq", None),
        P(None, "seq"),
        P("seq"),
        P(),
        P(),
        P("seq", "req"),
    )
    out_specs = (P("req", "seq", None), P("req", None, "seq"))
    return jax.shard_map(
        per_device, mesh=mesh, in_specs=in_specs, out_specs=out_specs, check_vma=False
    )
```

profile of v0, /device:TPU:0, one launch (start us, length us, event | category | flops | bytes accessed | tf_op | source)
XLA Modules:
  0.0 717.7 jit_solution(14593859675135900258)
XLA Ops:
  12.1 25.4 %all-gather.7.cloned.1.call-done = bf16[2,2048,256]{2,1,0:T(8,128)(2,1)} async-done(((bf16[2,256,256]{2,1,0:T(8,128)(2,1)}), bf16[2,2048,256]{2,1,0:T(8,128)(2,1)}) %all-gather.7.cloned.1.call-update) | async-done | bytes 2097168 | tf_op jit(solution)/shard_map/all_gather | solution.py:95
  39.2 72.3 %all-gather.5.cloned.1.call-done = bf16[2048,2048]{1,0:T(8,128)(2,1)} async-done(((bf16[128,2048]{1,0:T(8,128)(2,1)}), bf16[2048,2048]{1,0:T(8,128)(2,1)}) %all-gather.5.cloned.1.call-update) | async-done | bytes 8388624 | tf_op jit(solution)/shard_map/all_gather | solution.py:98
  111.5 6.9 fusion.33
  125.5 5.4 all-to-all-start.1
  132.2 88.7 %all-reduce.4.cloned.1.call-done = f32[2048,160]{0,1:T(8,128)} async-done(((f32[2048,160]{0,1:T(8,128)}), f32[2048,160]{0,1:T(8,128)}) %all-reduce.4.cloned.1.call-update) | async-done | bytes 1310736 | tf_op jit(solution)/shard_map/psum | solution.py:112
  225.0 5.1 all-to-all-start
  238.4 7.5 %all-to-all-done = bf16[16,128,256]{1,2,0:T(8,128)(2,1)S(1)} async-done(((bf16[16,128,256]{1,2,0:T(8,128)(2,1)}), bf16[16,128,256]{1,2,0:T(8,128)(2,1)S(1)}, u32[]{:S(2)}, u32[]{:S(2)}) %all-to-all-start) | async-done | bytes 1048608 | tf_op jit(solution)/shard_map/all_to_all | solution.py:124
  255.7 65.7 %while.35 = (s32[]{:T(128)}, f32[1,16,4096]{2,1,0:T(8,128)S(1)}, f32[16,1,8,4096]{3,2,1,0:T(8,128)}, f32[16,1,8,4096]{3,2,1,0:T(8,128)}, f32[16,4096]{1,0:T(8,12...) while((s32[]{:T(128)}, f32[1,16,4096]{2,1,0:T(8,128)S(1)}, ...), condition=%wide.region_11.12_spmd.clone, body=%wide.region_2.11_spmd.clone.sunk | while | flops 4849667 | bytes 4347896 | solution.py:51
  321.5 148.6 %while.33 = (s32[]{:T(128)}, f32[16,4096]{1,0:T(8,128)S(1)}, f32[1,16,4096]{2,1,0:T(8,128)S(1)}, f32[1,16,4096]{2,1,0:T(8,128)S(1)}, s32[]{:T(128)}) while((s32[]{:T(128)}, f32[16,4096]{1,0:T(8,128)S(1)}, f32[1,16,4096]{2,1,0:T(8,128)S(1)}, f32[1,16,4096]{2,1,0:T(8,128)S(1)}, s32[]{:T(128)}) %tuple.124), condition=%wide.region_13.14_spmd, body=%wide.region_12.13_spmd.sunk | while | flops 131074 | bytes 2097253 | solution.py:140
  328.0 4.4 collective-permute-start
  332.4 5.0 collective-permute-done
  337.4 4.4 collective-permute-start
  341.8 6.1 collective-permute-done
  352.4 6.1 collective-permute-done
  362.9 5.2 collective-permute-done
  385.2 6.8 collective-permute-start
  392.1 5.6 collective-permute-done
  397.7 6.2 collective-permute-start
  404.0 4.5 collective-permute-done
  408.5 5.6 collective-permute-start
  418.0 6.5 collective-permute-start
  428.4 6.5 collective-permute-start
  438.9 6.5 collective-permute-start
  449.3 6.5 collective-permute-start
  459.7 6.5 collective-permute-start
  471.6 35.8 %while.34 = (s32[]{:T(128)}, f32[16,1,8,4096]{3,2,1,0:T(8,128)}, f32[16,1,8,16]{3,2,1,0:T(8,128)S(1)}, f32[16,1,8,4096]{3,2,1,0:T(8,128)}, f32[16,4096]{1,0:T(8,128)S(1)}, /*index=5*/f32[16,4096]{1,0:T(8,128)S(1)}, s32[]{:T(128)}) while((s32[]{:T(128)}, f32[16,1,8,4096]{3,2,1,0:T(8,128)}, f32[16,1,8,16]{3,2,1,0:T(8,128)S(1)}, ...), condition=%wide.region_16.17_spmd, body=%wide.region_14.16_spmd.sunk | while | flops 2064386 | bytes 1312853 | solution.py:65
  512.9 18.0 %all-to-all-start.2 = ((bf16[128,16,256]{2,0,1:T(8,128)(2,1)}), bf16[128,16,256]{2,0,1:T(8,128)(2,1)S(1)}, u32[]{:S(2)}, u32[]{:S(2)}) async-start(bf16[128,16,256]{2,0,1:T(8,128)(2,1)} %fusion.30), calls=%async_computation.2 | async-start | bytes 2097152 | tf_op jit(solution)/shard_map/all_to_all | solution.py:147
  532.1 12.2 %all-to-all-done.2 = bf16[128,16,256]{2,0,1:T(8,128)(2,1)S(1)} async-done(((bf16[128,16,256]{2,0,1:T(8,128)(2,1)}), bf16[128,16,256]{2,0,1:T(8,128)(2,1)S(1)}, u32[]{:S(2)}, u32[]{:S(2)}) %all-to-all-start.2) | async-done | bytes 1048608 | tf_op jit(solution)/shard_map/all_to_all | solution.py:147
  546.7 6.8 convolution_convert_fusion
  554.1 66.1 %all-reduce.6.cloned.1.call-done = bf16[16,4096]{1,0:T(8,128)(2,1)} async-done(((bf16[16,4096]{1,0:T(8,128)(2,1)}), bf16[16,4096]{1,0:T(8,128)(2,1)}) %all-reduce.6.cloned.1.call-update) | async-done | bytes 131088 | tf_op jit(solution)/shard_map/psum | solution.py:18
  620.9 13.0 %all-gather = f32[128,256]{1,0:T(8,128)S(1)} all-gather(f32[16,256]{1,0:T(8,128)S(1)} %dynamic-slice_convert_fusion), channel_id=2, replica_groups=mesh['req'=8,'seq'=16] {'req'}, dimensions={0}, use_global_device_ids=true | all-gather | bytes 147456 | tf_op jit(solution)/shard_map/all_gather | solution.py:157
  634.6 74.3 %reduce-scatter.2.cloned.1.call-done = bf16[128,2048]{1,0:T(8,128)(2,1)} async-done(((bf16[2048,2048]{1,0:T(8,128)(2,1)}), bf16[128,2048]{1,0:T(8,128)(2,1)}) %reduce-scatter.2.cloned.1.call-update) | async-done | bytes 524304 | tf_op jit(solution)/shard_map/reduce_scatter | solution.py:151
  (356 shorter events, 207.6 us)
Async XLA Ops:
  7.2 115.5 %copy-start = (bf16[256,160]{0,1:T(8,128)(2,1)S(1)}, bf16[256,160]{0,1:T(8,128)(2,1)}, u32[]{:S(2)}) copy-start(bf16[256,160]{0,1:T(8,128)(2,1)} %param.26) | copy-start | bytes 245764
  7.2 30.3 %all-gather.7.cloned.1.call-start = ((), (), s32[]{:S(2)}) async-start(), calls=%async_computation.5 | async-start | bytes 2359296 | tf_op jit(solution)/shard_map/all_gather | solution.py:95
  7.9 103.6 %all-gather.5.cloned.1.call-start = ((), (), s32[]{:S(2)}) async-start(), calls=%async_computation.4 | async-start | bytes 8912896 | tf_op jit(solution)/shard_map/all_gather | solution.py:98
  12.0 209.0 %all-reduce.4.cloned.1.call-start = ((), (), s32[]{:S(2)}) async-start(), calls=%async_computation.6 | async-start | bytes 2621440 | tf_op jit(solution)/shard_map/psum | solution.py:112
  125.5 5.5 copy-start.14
  125.5 95.4 %copy-start.11 = (bf16[128,256]{1,0:T(8,128)(2,1)S(1)}, bf16[128,256]{1,0:T(8,128)(2,1)}, u32[]{:S(2)}) copy-start(bf16[128,256]{1,0:T(8,128)(2,1)} %param.27) | copy-start | bytes 196612
  125.5 99.5 %all-to-all-start.1 = ((bf16[16,128,256]{2,1,0:T(8,128)(2,1)}), bf16[16,128,256]{2,1,0:T(8,128)(2,1)S(1)}, u32[]{:S(2)}, u32[]{:S(2)}) async-start(bf16[16,128,256]{2,1,0:T(8,128)(2,1)} %bitcast.17), calls=%async_computation.1 | async-start | bytes 2097152 | tf_op jit(solution)/shard_map/all_to_all | solution.py:123
  223.6 7.1 copy-start.9
  225.0 20.9 %all-to-all-start = ((bf16[16,128,256]{1,2,0:T(8,128)(2,1)}), bf16[16,128,256]{1,2,0:T(8,128)(2,1)S(1)}, u32[]{:S(2)}, u32[]{:S(2)}) async-start(bf16[16,128,256]{1,2,0:T(8,128)(2,1)} %copy.43), calls=%async_computation | async-start | bytes 2097152 | tf_op jit(solution)/shard_map/all_to_all | solution.py:124
  230.1 316.6 %all-gather.9.cloned.1.call-start = ((), (), s32[]{:S(2)}) async-start(), calls=%async_computation.7 | async-start | bytes 1179648 | tf_op jit(solution)/shard_map/all_gather | solution.py:122
  321.5 6.4 collective-permute-start
  328.0 9.4 %collective-permute-start = (f32[16,4096]{1,0:T(8,128)S(1)}, f32[16,4096]{1,0:T(8,128)S(1)}, u32[]{:S(2)}, u32[]{:S(2)}) collective-permute-start(f32[16,4096]{1,0:T(8,128)S(1)} %bitcast_add_fusion.3), channel_id=1, source_target_pairs={{0,1},{1,2},{2,3},{3,4},{4,5},{5,6},{6,7},{7,8},{8,9},{9,10},{10,1... | collective-permute-start | bytes 786440 | tf_op jit(solution)/shard_map/while/body/eval_jaxpr/ppermute | solution.py:13
  337.4 10.5 %collective-permute-start = (f32[16,4096]{1,0:T(8,128)S(1)}, f32[16,4096]{1,0:T(8,128)S(1)}, u32[]{:S(2)}, u32[]{:S(2)}) collective-permute-start(f32[16,4096]{1,0:T(8,128)S(1)} %bitcast_add_fusion.3), channel_id=1, source_target_pairs={{0,1},{1,2},{2,3},{3,4},{4,5},{5,6},{6,7},{7,8},{8,9},{9,10},{10,1... | collective-permute-start | bytes 786440 | tf_op jit(solution)/shard_map/while/body/eval_jaxpr/ppermute | solution.py:13
  347.9 10.5 %collective-permute-start = (f32[16,4096]{1,0:T(8,128)S(1)}, f32[16,4096]{1,0:T(8,128)S(1)}, u32[]{:S(2)}, u32[]{:S(2)}) collective-permute-start(f32[16,4096]{1,0:T(8,128)S(1)} %bitcast_add_fusion.3), channel_id=1, source_target_pairs={{0,1},{1,2},{2,3},{3,4},{4,5},{5,6},{6,7},{7,8},{8,9},{9,10},{10,1... | collective-permute-start | bytes 786440 | tf_op jit(solution)/shard_map/while/body/eval_jaxpr/ppermute | solution.py:13
  358.5 9.6 %collective-permute-start = (f32[16,4096]{1,0:T(8,128)S(1)}, f32[16,4096]{1,0:T(8,128)S(1)}, u32[]{:S(2)}, u32[]{:S(2)}) collective-permute-start(f32[16,4096]{1,0:T(8,128)S(1)} %bitcast_add_fusion.3), channel_id=1, source_target_pairs={{0,1},{1,2},{2,3},{3,4},{4,5},{5,6},{6,7},{7,8},{8,9},{9,10},{10,1... | collective-permute-start | bytes 786440 | tf_op jit(solution)/shard_map/while/body/eval_jaxpr/ppermute | solution.py:13
  368.1 8.8 %collective-permute-start = (f32[16,4096]{1,0:T(8,128)S(1)}, f32[16,4096]{1,0:T(8,128)S(1)}, u32[]{:S(2)}, u32[]{:S(2)}) collective-permute-start(f32[16,4096]{1,0:T(8,128)S(1)} %bitcast_add_fusion.3), channel_id=1, source_target_pairs={{0,1},{1,2},{2,3},{3,4},{4,5},{5,6},{6,7},{7,8},{8,9},{9,10},{10,1... | collective-permute-start | bytes 786440 | tf_op jit(solution)/shard_map/while/body/eval_jaxpr/ppermute | solution.py:13
  376.9 8.3 %collective-permute-start = (f32[16,4096]{1,0:T(8,128)S(1)}, f32[16,4096]{1,0:T(8,128)S(1)}, u32[]{:S(2)}, u32[]{:S(2)}) collective-permute-start(f32[16,4096]{1,0:T(8,128)S(1)} %bitcast_add_fusion.3), channel_id=1, source_target_pairs={{0,1},{1,2},{2,3},{3,4},{4,5},{5,6},{6,7},{7,8},{8,9},{9,10},{10,1... | collective-permute-start | bytes 786440 | tf_op jit(solution)/shard_map/while/body/eval_jaxpr/ppermute | solution.py:13
  385.2 12.5 %collective-permute-start = (f32[16,4096]{1,0:T(8,128)S(1)}, f32[16,4096]{1,0:T(8,128)S(1)}, u32[]{:S(2)}, u32[]{:S(2)}) collective-permute-start(f32[16,4096]{1,0:T(8,128)S(1)} %bitcast_add_fusion.3), channel_id=1, source_target_pairs={{0,1},{1,2},{2,3},{3,4},{4,5},{5,6},{6,7},{7,8},{8,9},{9,10},{10,1... | collective-permute-start | bytes 786440 | tf_op jit(solution)/shard_map/while/body/eval_jaxpr/ppermute | solution.py:13
  397.7 10.7 %collective-permute-start = (f32[16,4096]{1,0:T(8,128)S(1)}, f32[16,4096]{1,0:T(8,128)S(1)}, u32[]{:S(2)}, u32[]{:S(2)}) collective-permute-start(f32[16,4096]{1,0:T(8,128)S(1)} %bitcast_add_fusion.3), channel_id=1, source_target_pairs={{0,1},{1,2},{2,3},{3,4},{4,5},{5,6},{6,7},{7,8},{8,9},{9,10},{10,1... | collective-permute-start | bytes 786440 | tf_op jit(solution)/shard_map/while/body/eval_jaxpr/ppermute | solution.py:13
  408.5 9.5 %collective-permute-start = (f32[16,4096]{1,0:T(8,128)S(1)}, f32[16,4096]{1,0:T(8,128)S(1)}, u32[]{:S(2)}, u32[]{:S(2)}) collective-permute-start(f32[16,4096]{1,0:T(8,128)S(1)} %bitcast_add_fusion.3), channel_id=1, source_target_pairs={{0,1},{1,2},{2,3},{3,4},{4,5},{5,6},{6,7},{7,8},{8,9},{9,10},{10,1... | collective-permute-start | bytes 786440 | tf_op jit(solution)/shard_map/while/body/eval_jaxpr/ppermute | solution.py:13
  418.0 10.4 %collective-permute-start = (f32[16,4096]{1,0:T(8,128)S(1)}, f32[16,4096]{1,0:T(8,128)S(1)}, u32[]{:S(2)}, u32[]{:S(2)}) collective-permute-start(f32[16,4096]{1,0:T(8,128)S(1)} %bitcast_add_fusion.3), channel_id=1, source_target_pairs={{0,1},{1,2},{2,3},{3,4},{4,5},{5,6},{6,7},{7,8},{8,9},{9,10},{10,1... | collective-permute-start | bytes 786440 | tf_op jit(solution)/shard_map/while/body/eval_jaxpr/ppermute | solution.py:13
  428.4 10.4 %collective-permute-start = (f32[16,4096]{1,0:T(8,128)S(1)}, f32[16,4096]{1,0:T(8,128)S(1)}, u32[]{:S(2)}, u32[]{:S(2)}) collective-permute-start(f32[16,4096]{1,0:T(8,128)S(1)} %bitcast_add_fusion.3), channel_id=1, source_target_pairs={{0,1},{1,2},{2,3},{3,4},{4,5},{5,6},{6,7},{7,8},{8,9},{9,10},{10,1... | collective-permute-start | bytes 786440 | tf_op jit(solution)/shard_map/while/body/eval_jaxpr/ppermute | solution.py:13
  438.9 10.4 %collective-permute-start = (f32[16,4096]{1,0:T(8,128)S(1)}, f32[16,4096]{1,0:T(8,128)S(1)}, u32[]{:S(2)}, u32[]{:S(2)}) collective-permute-start(f32[16,4096]{1,0:T(8,128)S(1)} %bitcast_add_fusion.3), channel_id=1, source_target_pairs={{0,1},{1,2},{2,3},{3,4},{4,5},{5,6},{6,7},{7,8},{8,9},{9,10},{10,1... | collective-permute-start | bytes 786440 | tf_op jit(solution)/shard_map/while/body/eval_jaxpr/ppermute | solution.py:13
  449.3 10.4 %collective-permute-start = (f32[16,4096]{1,0:T(8,128)S(1)}, f32[16,4096]{1,0:T(8,128)S(1)}, u32[]{:S(2)}, u32[]{:S(2)}) collective-permute-start(f32[16,4096]{1,0:T(8,128)S(1)} %bitcast_add_fusion.3), channel_id=1, source_target_pairs={{0,1},{1,2},{2,3},{3,4},{4,5},{5,6},{6,7},{7,8},{8,9},{9,10},{10,1... | collective-permute-start | bytes 786440 | tf_op jit(solution)/shard_map/while/body/eval_jaxpr/ppermute | solution.py:13
  459.7 10.4 %collective-permute-start = (f32[16,4096]{1,0:T(8,128)S(1)}, f32[16,4096]{1,0:T(8,128)S(1)}, u32[]{:S(2)}, u32[]{:S(2)}) collective-permute-start(f32[16,4096]{1,0:T(8,128)S(1)} %bitcast_add_fusion.3), channel_id=1, source_target_pairs={{0,1},{1,2},{2,3},{3,4},{4,5},{5,6},{6,7},{7,8},{8,9},{9,10},{10,1... | collective-permute-start | bytes 786440 | tf_op jit(solution)/shard_map/while/body/eval_jaxpr/ppermute | solution.py:13
  512.9 18.1 %copy-start.5 = (f32[16,4096]{1,0:T(8,128)S(1)}, f32[16,4096]{1,0:T(8,128)}, u32[]{:S(2)}) copy-start(f32[16,4096]{1,0:T(8,128)} %param.29) | copy-start | bytes 786436
  512.9 18.1 %copy-start.7 = (f32[1,1,4096]{2,1,0:T(1,128)S(1)}, f32[1,1,4096]{2,1,0:T(1,128)}, u32[]{:S(2)}) copy-start(f32[1,1,4096]{2,1,0:T(1,128)} %copy-done.6) | copy-start | bytes 49156
  512.9 31.4 %all-to-all-start.2 = ((bf16[128,16,256]{2,0,1:T(8,128)(2,1)}), bf16[128,16,256]{2,0,1:T(8,128)(2,1)S(1)}, u32[]{:S(2)}, u32[]{:S(2)}) async-start(bf16[128,16,256]{2,0,1:T(8,128)(2,1)} %fusion.30), calls=%async_computation.2 | async-start | bytes 2097152 | tf_op jit(solution)/shard_map/all_to_all | solution.py:147
  531.0 89.2 %all-reduce.6.cloned.1.call-start = ((), (), s32[]{:S(2)}) async-start(), calls=%async_computation.9 | async-start | bytes 262144 | tf_op jit(solution)/shard_map/psum | solution.py:18
  531.8 177.1 %reduce-scatter.2.cloned.1.call-start = ((), (), s32[]{:S(2)}) async-start(), calls=%async_computation.8 | async-start | bytes 8912896 | tf_op jit(solution)/shard_map/reduce_scatter | solution.py:151
  553.5 155.5 %copy-start.2 = (bf16[1,128,2048]{2,1,0:T(8,128)(2,1)S(1)}, bf16[1,128,2048]{2,1,0:T(8,128)(2,1)}, u32[]{:S(2)}) copy-start(bf16[1,128,2048]{2,1,0:T(8,128)(2,1)} %param.19) | copy-start | bytes 1572868
  553.5 157.4 %copy-start.1 = (bf16[256,160]{0,1:T(8,128)(2,1)S(1)}, bf16[256,160]{0,1:T(8,128)(2,1)}, u32[]{:S(2)}) copy-start(bf16[256,160]{0,1:T(8,128)(2,1)} %param.26) | copy-start | bytes 245764
  (8 other events, 25.3 us)
Sparse Core Ops, SparseCore 0:
  9.7 27.7 all-gather.6
  40.2 71.2 all-gather.4
  125.6 95.2 all-reduce.3
  232.3 24.7 all-gather.8
  535.2 84.9 all-reduce.5
  623.5 85.3 reduce-scatter.1
where the time goes:
time: 720 us; the launch traced here: 718 us
  waiting for transfers between devices  415 us (58%)
  starting transfers between devices  109 us (15%)
  local copies, waits for them, and re-layouts  89.9 us (12%)
  other arithmetic  54.7 us (8%)
  matrix products  19.6 us (3%)
  between operations  14.4 us (2%)
  blocking collectives  13 us (2%)
    psum x1, waiting for transfers between devices, per_device(): summed = lax.psum(partial_proj, 'seq')  88.7 us
    ppermute x15, starting transfers between devices, shifted(): return lax.ppermute(block, axis, route)  80.1 us
    reduce_scatter x1, waiting for transfers between devices, per_device(): lax.psum_scatter(jnp.dot(gated_ch, w_out, preferred_element_type=jnp.floa...  74.3 us
    all_gather x1, waiting for transfers between devices, per_device(): lax.all_gather(normed, 'seq', axis=0, tiled=True)  72.3 us
    ppermute x15, waiting for transfers between devices, shifted(): return lax.ppermute(block, axis, route)  67.6 us
    psum x1, waiting for transfers between devices, spread(): return lax.psum(jnp.where(mine, array, jnp.zeros_like(array)), axis)  66.1 us
    squeeze x32, local copies, waits for them, and re-layouts, piece_scan(): lax.scan(advance, start, (to_blocks(rates), to_blocks(values), to_blocks(...  26.9 us
    all_gather x1, waiting for transfers between devices, per_device(): w_in = lax.all_gather(in_weight, 'req', axis=1, tiled=True)  25.4 us
  transfers between devices with their start and end apart: 24, of which 22 were waited for; matrix products, arithmetic and copies ran while one was open for 20% of the time, Pallas kernels for 0%

commit v1 on v0

--- a/solution.py
+++ b/solution.py
@@ -109,7 +109,7 @@
     inner = jax.nn.silu(convolved).astype(jnp.bfloat16)
     partial_proj = jnp.dot(inner, xproj_weight, preferred_element_type=jnp.float32)
     length_here = lax.dynamic_index_in_dim(lengths, req_index, 0, keepdims=False)
-    summed = lax.psum(partial_proj, "seq")
+    summed = jnp.sum(lax.all_gather(partial_proj, "seq"), axis=0)
     live_all = (jnp.arange(span, dtype=jnp.int32) < length_here).astype(jnp.float32)
     rate_low = summed[:, :RANK].astype(jnp.bfloat16)
     delta_ch = (

time: 720 us -> 788 us (1.094)
  waiting for transfers between devices: 415 us -> 458 us
  local copies, waits for them, and re-layouts: 89.9 us -> 109 us
    all_gather x0 -> x1, waiting for transfers between devices: none -> 132 us  [per_device(): summed = jnp.sum(lax.all_gather(partial_proj, 'seq'), axis=0)]
    psum x1 -> x0, waiting for transfers between devices: 88.7 us -> none  [per_device(): summed = lax.psum(partial_proj, 'seq')]
    unnamed x33 -> x36, local copies, waits for them, and re-layouts: 4.42 us -> 23.2 us
  transfers between devices with their start and end apart: 24 -> 24, of which waited for: 22 -> 22; matrix products, arithmetic and copies ran while one was open for 20% -> 22% of each run, Pallas kernels for 0% -> 0%
where the time goes in v1:
time: 788 us; the launch traced here: 786 us
  waiting for transfers between devices  458 us (58%)
  starting transfers between devices  111 us (14%)
  local copies, waits for them, and re-layouts  109 us (14%)
  other arithmetic  59.8 us (8%)
  matrix products  18.5 us (2%)
  between operations  14.5 us (2%)
  blocking collectives  13 us (2%)
    all_gather x1, waiting for transfers between devices, per_device(): summed = jnp.sum(lax.all_gather(partial_proj, 'seq'), axis=0)  132 us
    ppermute x15, starting transfers between devices, shifted(): return lax.ppermute(block, axis, route)  82.2 us
    reduce_scatter x1, waiting for transfers between devices, per_device(): lax.psum_scatter(jnp.dot(gated_ch, w_out, preferred_element_type=jnp.floa...  74.3 us
    all_gather x1, waiting for transfers between devices, per_device(): lax.all_gather(normed, 'seq', axis=0, tiled=True)  72.3 us
    psum x1, waiting for transfers between devices, spread(): return lax.psum(jnp.where(mine, array, jnp.zeros_like(array)), axis)  66.2 us
    ppermute x15, waiting for transfers between devices, shifted(): return lax.ppermute(block, axis, route)  65.7 us
    squeeze x32, local copies, waits for them, and re-layouts, piece_scan(): lax.scan(advance, start, (to_blocks(rates), to_blocks(values), to_blocks(...  26.9 us
    all_gather x1, waiting for transfers between devices, per_device(): w_in = lax.all_gather(in_weight, 'req', axis=1, tiled=True)  25.4 us
  transfers between devices with their start and end apart: 24, of which 22 were waited for; matrix products, arithmetic and copies ran while one was open for 22% of the time, Pallas kernels for 0%

profile of v1, /device:TPU:0, one launch (start us, length us, event | category | flops | bytes accessed | tf_op | source)
XLA Modules:
  0.0 785.6 jit_solution(3152464345115488834)
XLA Ops:
  12.1 25.4 %all-gather.9.cloned.1.call-done = bf16[2,2048,256]{2,1,0:T(8,128)(2,1)} async-done(((bf16[2,256,256]{2,1,0:T(8,128)(2,1)}), bf16[2,2048,256]{2,1,0:T(8,128)(2,1)}) %all-gather.9.cloned.1.call-update) | async-done | bytes 2097168 | tf_op jit(solution)/shard_map/all_gather | solution.py:95
  39.2 72.3 %all-gather.7.cloned.1.call-done = bf16[2048,2048]{1,0:T(8,128)(2,1)} async-done(((bf16[128,2048]{1,0:T(8,128)(2,1)}), bf16[2048,2048]{1,0:T(8,128)(2,1)}) %all-gather.7.cloned.1.call-update) | async-done | bytes 8388624 | tf_op jit(solution)/shard_map/all_gather | solution.py:98
  111.5 6.9 fusion.33
  126.9 5.3 all-to-all-start.1
  132.2 131.8 %all-gather.13.cloned.1.call-done = f32[32768,160]{0,1:T(8,128)} async-done(((f32[2048,160]{0,1:T(8,128)}), f32[32768,160]{0,1:T(8,128)}) %all-gather.13.cloned.1.call-update) | async-done | bytes 20971536 | tf_op jit(solution)/shard_map/all_gather | solution.py:112
  264.0 18.8 %copy.61 = f32[20,8,16,2048]{3,2,1,0:T(8,128)S(1)} copy(f32[20,8,16,2048]{3,1,2,0:T(8,128)} %bitcast.317) | data formatting | bytes 41943040
  282.8 5.1 bitcast_reduce_fusion
  290.8 5.3 all-to-all-start
  304.4 9.2 %all-to-all-done = bf16[16,128,256]{1,2,0:T(8,128)(2,1)S(1)} async-done(((bf16[16,128,256]{1,2,0:T(8,128)(2,1)}), bf16[16,128,256]{1,2,0:T(8,128)(2,1)S(1)}, u32[]{:S(2)}, u32[]{:S(2)}) %all-to-all-start) | async-done | bytes 1048608 | tf_op jit(solution)/shard_map/all_to_all | solution.py:124
  323.4 65.9 %while.35 = (s32[]{:T(128)}, f32[1,16,4096]{2,1,0:T(8,128)S(1)}, f32[16,1,8,4096]{3,2,1,0:T(8,128)}, f32[16,1,8,4096]{3,2,1,0:T(8,128)}, f32[16,4096]{1,0:T(8,12...) while((s32[]{:T(128)}, f32[1,16,4096]{2,1,0:T(8,128)S(1)}, ...), condition=%wide.region_11.12_spmd.clone, body=%wide.region_2.11_spmd.clone.sunk | while | flops 4849667 | bytes 4347896 | solution.py:51
  389.3 148.8 %while.33 = (s32[]{:T(128)}, f32[16,4096]{1,0:T(8,128)S(1)}, f32[1,16,4096]{2,1,0:T(8,128)S(1)}, f32[1,16,4096]{2,1,0:T(8,128)S(1)}, s32[]{:T(128)}) while((s32[]{:T(128)}, f32[16,4096]{1,0:T(8,128)S(1)}, f32[1,16,4096]{2,1,0:T(8,128)S(1)}, f32[1,16,4096]{2,1,0:T(8,128)S(1)}, s32[]{:T(128)}) %tuple.127), condition=%wide.region_13.14_spmd, body=%wide.region_12.13_spmd.sunk | while | flops 131074 | bytes 2097253 | solution.py:140
  433.5 4.6 collective-permute-done
  438.2 6.0 collective-permute-start
  444.2 5.4 collective-permute-done
  449.6 7.2 collective-permute-start
  456.8 6.5 collective-permute-done
  463.4 7.1 collective-permute-start
  470.5 5.6 collective-permute-done
  476.2 6.2 collective-permute-start
  482.4 4.5 collective-permute-done
  486.9 5.6 collective-permute-start
  496.5 6.5 collective-permute-start
  506.9 6.5 collective-permute-start
  517.3 6.5 collective-permute-start
  527.7 6.5 collective-permute-start
  539.6 35.9 %while.34 = (s32[]{:T(128)}, f32[16,1,8,4096]{3,2,1,0:T(8,128)}, f32[16,1,8,16]{3,2,1,0:T(8,128)S(1)}, f32[16,1,8,4096]{3,2,1,0:T(8,128)}, f32[16,4096]{1,0:T(8,128)S(1)}, /*index=5*/f32[16,4096]{1,0:T(8,128)S(1)}, s32[]{:T(128)}) while((s32[]{:T(128)}, f32[16,1,8,4096]{3,2,1,0:T(8,128)}, f32[16,1,8,16]{3,2,1,0:T(8,128)S(1)}, ...), condition=%wide.region_16.17_spmd, body=%wide.region_14.16_spmd.sunk | while | flops 2064386 | bytes 1312853 | solution.py:65
  581.0 17.7 %all-to-all-start.2 = ((bf16[128,16,256]{2,0,1:T(8,128)(2,1)}), bf16[128,16,256]{2,0,1:T(8,128)(2,1)S(1)}, u32[]{:S(2)}, u32[]{:S(2)}) async-start(bf16[128,16,256]{2,0,1:T(8,128)(2,1)} %fusion.30), calls=%async_computation.2 | async-start | bytes 2097152 | tf_op jit(solution)/shard_map/all_to_all | solution.py:147
  599.8 12.2 %all-to-all-done.2 = bf16[128,16,256]{2,0,1:T(8,128)(2,1)S(1)} async-done(((bf16[128,16,256]{2,0,1:T(8,128)(2,1)}), bf16[128,16,256]{2,0,1:T(8,128)(2,1)S(1)}, u32[]{:S(2)}, u32[]{:S(2)}) %all-to-all-start.2) | async-done | bytes 1048608 | tf_op jit(solution)/shard_map/all_to_all | solution.py:147
  614.4 6.8 convolution_convert_fusion
  621.9 66.2 %all-reduce.3.cloned.1.call-done = bf16[16,4096]{1,0:T(8,128)(2,1)} async-done(((bf16[16,4096]{1,0:T(8,128)(2,1)}), bf16[16,4096]{1,0:T(8,128)(2,1)}) %all-reduce.3.cloned.1.call-update) | async-done | bytes 131088 | tf_op jit(solution)/shard_map/psum | solution.py:18
  688.8 13.0 %all-gather.1 = f32[128,256]{1,0:T(8,128)S(1)} all-gather(f32[16,256]{1,0:T(8,128)S(1)} %dynamic-slice_convert_fusion), channel_id=3, replica_groups=mesh['req'=8,'seq'=16] {'req'}, dimensions={0}, use_global_device_ids=true | all-gather | bytes 147456 | tf_op jit(solution)/shard_map/all_gather | solution.py:157
  702.5 74.3 %reduce-scatter.2.cloned.1.call-done = bf16[128,2048]{1,0:T(8,128)(2,1)} async-done(((bf16[2048,2048]{1,0:T(8,128)(2,1)}), bf16[128,2048]{1,0:T(8,128)(2,1)}) %reduce-scatter.2.cloned.1.call-update) | async-done | bytes 524304 | tf_op jit(solution)/shard_map/reduce_scatter | solution.py:151
  (360 shorter events, 214.4 us)
Async XLA Ops:
  7.2 115.5 %copy-start = (bf16[256,160]{0,1:T(8,128)(2,1)S(1)}, bf16[256,160]{0,1:T(8,128)(2,1)}, u32[]{:S(2)}) copy-start(bf16[256,160]{0,1:T(8,128)(2,1)} %param.26) | copy-start | bytes 245764
  7.2 30.3 %all-gather.9.cloned.1.call-start = ((), (), s32[]{:S(2)}) async-start(), calls=%async_computation.5 | async-start | bytes 2359296 | tf_op jit(solution)/shard_map/all_gather | solution.py:95
  7.9 103.6 %all-gather.7.cloned.1.call-start = ((), (), s32[]{:S(2)}) async-start(), calls=%async_computation.4 | async-start | bytes 8912896 | tf_op jit(solution)/shard_map/all_gather | solution.py:98
  12.0 252.1 %all-gather.13.cloned.1.call-start = ((), (), s32[]{:S(2)}) async-start(), calls=%async_computation.9 | async-start | bytes 22282240 | tf_op jit(solution)/shard_map/all_gather | solution.py:112
  126.9 163.9 %all-to-all-start.1 = ((bf16[16,128,256]{2,1,0:T(8,128)(2,1)}), bf16[16,128,256]{2,1,0:T(8,128)(2,1)S(1)}, u32[]{:S(2)}, u32[]{:S(2)}) async-start(bf16[16,128,256]{2,1,0:T(8,128)(2,1)} %bitcast.17), calls=%async_computation.1 | async-start | bytes 2097152 | tf_op jit(solution)/shard_map/all_to_all | solution.py:123
  282.8 5.1 copy-start.12
  289.5 7.2 copy-start.10
  290.8 22.8 %all-to-all-start = ((bf16[16,128,256]{1,2,0:T(8,128)(2,1)}), bf16[16,128,256]{1,2,0:T(8,128)(2,1)S(1)}, u32[]{:S(2)}, u32[]{:S(2)}) async-start(bf16[16,128,256]{1,2,0:T(8,128)(2,1)} %copy.50), calls=%async_computation | async-start | bytes 2097152 | tf_op jit(solution)/shard_map/all_to_all | solution.py:124
  296.1 318.3 %all-gather.11.cloned.1.call-start = ((), (), s32[]{:S(2)}) async-start(), calls=%async_computation.6 | async-start | bytes 1179648 | tf_op jit(solution)/shard_map/all_gather | solution.py:122
  315.4 5.4 copy-start.7
  389.4 6.0 collective-permute-start
  395.4 8.5 %collective-permute-start = (f32[16,4096]{1,0:T(8,128)S(1)}, f32[16,4096]{1,0:T(8,128)S(1)}, u32[]{:S(2)}, u32[]{:S(2)}) collective-permute-start(f32[16,4096]{1,0:T(8,128)S(1)} %bitcast_add_fusion.3), channel_id=1, source_target_pairs={{0,1},{1,2},{2,3},{3,4},{4,5},{5,6},{6,7},{7,8},{8,9},{9,10},{10,1... | collective-permute-start | bytes 786440 | tf_op jit(solution)/shard_map/while/body/eval_jaxpr/ppermute | solution.py:13
  404.0 8.3 %collective-permute-start = (f32[16,4096]{1,0:T(8,128)S(1)}, f32[16,4096]{1,0:T(8,128)S(1)}, u32[]{:S(2)}, u32[]{:S(2)}) collective-permute-start(f32[16,4096]{1,0:T(8,128)S(1)} %bitcast_add_fusion.3), channel_id=1, source_target_pairs={{0,1},{1,2},{2,3},{3,4},{4,5},{5,6},{6,7},{7,8},{8,9},{9,10},{10,1... | collective-permute-start | bytes 786440 | tf_op jit(solution)/shard_map/while/body/eval_jaxpr/ppermute | solution.py:13
  412.3 8.3 %collective-permute-start = (f32[16,4096]{1,0:T(8,128)S(1)}, f32[16,4096]{1,0:T(8,128)S(1)}, u32[]{:S(2)}, u32[]{:S(2)}) collective-permute-start(f32[16,4096]{1,0:T(8,128)S(1)} %bitcast_add_fusion.3), channel_id=1, source_target_pairs={{0,1},{1,2},{2,3},{3,4},{4,5},{5,6},{6,7},{7,8},{8,9},{9,10},{10,1... | collective-permute-start | bytes 786440 | tf_op jit(solution)/shard_map/while/body/eval_jaxpr/ppermute | solution.py:13
  420.6 8.4 %collective-permute-start = (f32[16,4096]{1,0:T(8,128)S(1)}, f32[16,4096]{1,0:T(8,128)S(1)}, u32[]{:S(2)}, u32[]{:S(2)}) collective-permute-start(f32[16,4096]{1,0:T(8,128)S(1)} %bitcast_add_fusion.3), channel_id=1, source_target_pairs={{0,1},{1,2},{2,3},{3,4},{4,5},{5,6},{6,7},{7,8},{8,9},{9,10},{10,1... | collective-permute-start | bytes 786440 | tf_op jit(solution)/shard_map/while/body/eval_jaxpr/ppermute | solution.py:13
  429.1 9.1 %collective-permute-start = (f32[16,4096]{1,0:T(8,128)S(1)}, f32[16,4096]{1,0:T(8,128)S(1)}, u32[]{:S(2)}, u32[]{:S(2)}) collective-permute-start(f32[16,4096]{1,0:T(8,128)S(1)} %bitcast_add_fusion.3), channel_id=1, source_target_pairs={{0,1},{1,2},{2,3},{3,4},{4,5},{5,6},{6,7},{7,8},{8,9},{9,10},{10,1... | collective-permute-start | bytes 786440 | tf_op jit(solution)/shard_map/while/body/eval_jaxpr/ppermute | solution.py:13
  438.2 11.4 %collective-permute-start = (f32[16,4096]{1,0:T(8,128)S(1)}, f32[16,4096]{1,0:T(8,128)S(1)}, u32[]{:S(2)}, u32[]{:S(2)}) collective-permute-start(f32[16,4096]{1,0:T(8,128)S(1)} %bitcast_add_fusion.3), channel_id=1, source_target_pairs={{0,1},{1,2},{2,3},{3,4},{4,5},{5,6},{6,7},{7,8},{8,9},{9,10},{10,1... | collective-permute-start | bytes 786440 | tf_op jit(solution)/shard_map/while/body/eval_jaxpr/ppermute | solution.py:13
  449.6 13.8 %collective-permute-start = (f32[16,4096]{1,0:T(8,128)S(1)}, f32[16,4096]{1,0:T(8,128)S(1)}, u32[]{:S(2)}, u32[]{:S(2)}) collective-permute-start(f32[16,4096]{1,0:T(8,128)S(1)} %bitcast_add_fusion.3), channel_id=1, source_target_pairs={{0,1},{1,2},{2,3},{3,4},{4,5},{5,6},{6,7},{7,8},{8,9},{9,10},{10,1... | collective-permute-start | bytes 786440 | tf_op jit(solution)/shard_map/while/body/eval_jaxpr/ppermute | solution.py:13
  463.4 12.7 %collective-permute-start = (f32[16,4096]{1,0:T(8,128)S(1)}, f32[16,4096]{1,0:T(8,128)S(1)}, u32[]{:S(2)}, u32[]{:S(2)}) collective-permute-start(f32[16,4096]{1,0:T(8,128)S(1)} %bitcast_add_fusion.3), channel_id=1, source_target_pairs={{0,1},{1,2},{2,3},{3,4},{4,5},{5,6},{6,7},{7,8},{8,9},{9,10},{10,1... | collective-permute-start | bytes 786440 | tf_op jit(solution)/shard_map/while/body/eval_jaxpr/ppermute | solution.py:13
  476.2 10.7 %collective-permute-start = (f32[16,4096]{1,0:T(8,128)S(1)}, f32[16,4096]{1,0:T(8,128)S(1)}, u32[]{:S(2)}, u32[]{:S(2)}) collective-permute-start(f32[16,4096]{1,0:T(8,128)S(1)} %bitcast_add_fusion.3), channel_id=1, source_target_pairs={{0,1},{1,2},{2,3},{3,4},{4,5},{5,6},{6,7},{7,8},{8,9},{9,10},{10,1... | collective-permute-start | bytes 786440 | tf_op jit(solution)/shard_map/while/body/eval_jaxpr/ppermute | solution.py:13
  486.9 9.5 %collective-permute-start = (f32[16,4096]{1,0:T(8,128)S(1)}, f32[16,4096]{1,0:T(8,128)S(1)}, u32[]{:S(2)}, u32[]{:S(2)}) collective-permute-start(f32[16,4096]{1,0:T(8,128)S(1)} %bitcast_add_fusion.3), channel_id=1, source_target_pairs={{0,1},{1,2},{2,3},{3,4},{4,5},{5,6},{6,7},{7,8},{8,9},{9,10},{10,1... | collective-permute-start | bytes 786440 | tf_op jit(solution)/shard_map/while/body/eval_jaxpr/ppermute | solution.py:13
  496.5 10.4 %collective-permute-start = (f32[16,4096]{1,0:T(8,128)S(1)}, f32[16,4096]{1,0:T(8,128)S(1)}, u32[]{:S(2)}, u32[]{:S(2)}) collective-permute-start(f32[16,4096]{1,0:T(8,128)S(1)} %bitcast_add_fusion.3), channel_id=1, source_target_pairs={{0,1},{1,2},{2,3},{3,4},{4,5},{5,6},{6,7},{7,8},{8,9},{9,10},{10,1... | collective-permute-start | bytes 786440 | tf_op jit(solution)/shard_map/while/body/eval_jaxpr/ppermute | solution.py:13
  506.9 10.4 %collective-permute-start = (f32[16,4096]{1,0:T(8,128)S(1)}, f32[16,4096]{1,0:T(8,128)S(1)}, u32[]{:S(2)}, u32[]{:S(2)}) collective-permute-start(f32[16,4096]{1,0:T(8,128)S(1)} %bitcast_add_fusion.3), channel_id=1, source_target_pairs={{0,1},{1,2},{2,3},{3,4},{4,5},{5,6},{6,7},{7,8},{8,9},{9,10},{10,1... | collective-permute-start | bytes 786440 | tf_op jit(solution)/shard_map/while/body/eval_jaxpr/ppermute | solution.py:13
  517.3 10.4 %collective-permute-start = (f32[16,4096]{1,0:T(8,128)S(1)}, f32[16,4096]{1,0:T(8,128)S(1)}, u32[]{:S(2)}, u32[]{:S(2)}) collective-permute-start(f32[16,4096]{1,0:T(8,128)S(1)} %bitcast_add_fusion.3), channel_id=1, source_target_pairs={{0,1},{1,2},{2,3},{3,4},{4,5},{5,6},{6,7},{7,8},{8,9},{9,10},{10,1... | collective-permute-start | bytes 786440 | tf_op jit(solution)/shard_map/while/body/eval_jaxpr/ppermute | solution.py:13
  527.7 10.4 %collective-permute-start = (f32[16,4096]{1,0:T(8,128)S(1)}, f32[16,4096]{1,0:T(8,128)S(1)}, u32[]{:S(2)}, u32[]{:S(2)}) collective-permute-start(f32[16,4096]{1,0:T(8,128)S(1)} %bitcast_add_fusion.3), channel_id=1, source_target_pairs={{0,1},{1,2},{2,3},{3,4},{4,5},{5,6},{6,7},{7,8},{8,9},{9,10},{10,1... | collective-permute-start | bytes 786440 | tf_op jit(solution)/shard_map/while/body/eval_jaxpr/ppermute | solution.py:13
  581.0 17.8 %copy-start.6 = (f32[16,4096]{1,0:T(8,128)S(1)}, f32[16,4096]{1,0:T(8,128)}, u32[]{:S(2)}) copy-start(f32[16,4096]{1,0:T(8,128)} %param.29) | copy-start | bytes 786436
  581.0 17.8 %copy-start.8 = (f32[1,1,4096]{2,1,0:T(1,128)S(1)}, f32[1,1,4096]{2,1,0:T(1,128)}, u32[]{:S(2)}) copy-start(f32[1,1,4096]{2,1,0:T(1,128)} %copy-done.7) | copy-start | bytes 49156
  581.0 31.0 %all-to-all-start.2 = ((bf16[128,16,256]{2,0,1:T(8,128)(2,1)}), bf16[128,16,256]{2,0,1:T(8,128)(2,1)S(1)}, u32[]{:S(2)}, u32[]{:S(2)}) async-start(bf16[128,16,256]{2,0,1:T(8,128)(2,1)} %fusion.30), calls=%async_computation.2 | async-start | bytes 2097152 | tf_op jit(solution)/shard_map/all_to_all | solution.py:147
  598.7 89.4 %all-reduce.3.cloned.1.call-start = ((), (), s32[]{:S(2)}) async-start(), calls=%async_computation.8 | async-start | bytes 262144 | tf_op jit(solution)/shard_map/psum | solution.py:18
  599.6 177.2 %reduce-scatter.2.cloned.1.call-start = ((), (), s32[]{:S(2)}) async-start(), calls=%async_computation.7 | async-start | bytes 8912896 | tf_op jit(solution)/shard_map/reduce_scatter | solution.py:151
  621.2 155.6 %copy-start.2 = (bf16[1,128,2048]{2,1,0:T(8,128)(2,1)S(1)}, bf16[1,128,2048]{2,1,0:T(8,128)(2,1)}, u32[]{:S(2)}) copy-start(bf16[1,128,2048]{2,1,0:T(8,128)(2,1)} %param.19) | copy-start | bytes 1572868
  621.3 157.5 %copy-start.1 = (bf16[256,160]{0,1:T(8,128)(2,1)S(1)}, bf16[256,160]{0,1:T(8,128)(2,1)}, u32[]{:S(2)}) copy-start(bf16[256,160]{0,1:T(8,128)(2,1)} %param.26) | copy-start | bytes 245764
  (9 other events, 21.7 us)
Sparse Core Ops, SparseCore 0:
  9.7 27.7 all-gather.8
  40.2 71.2 all-gather.6
  125.7 138.2 all-gather.12
  298.3 24.7 all-gather.10
  603.0 85.0 all-reduce.2
  691.4 85.3 reduce-scatter.1
